TPU v7x, 32 devices: a whole 2x2x4 slice. The times are simulated.
32 devices in a mesh: dp: 4 (over y, core), row: 2 (over x), col: 4 (over z).
Axes of the slice: x: 2, y: 2, z: 4, core: 2. Of those that a mesh axis runs over, the one named last changes fastest.
Arguments:
- block_in: bfloat16 [8192, 1536], P(('dp', 'row', 'col')), may hold values from -6 to 6
- out_grad: bfloat16 [8192, 1536], P(('dp', 'row', 'col')), may hold values from -6 to 6
- norm_gain: float32 [1536], replicated, may hold values from 0.5 to 1.5
- first_norm_gain: float32 [1536], replicated, may hold values from -28 to 28
- second_norm_gain: float32 [1536], replicated, may hold values from 16.384 to 163.84
- input_proj: float32 [1536, 6144], P('dp', ('row', 'col')), may hold values from -0.18371173 to 0.18371173
- first_input_proj: float32 [1536, 6144], P('dp', ('row', 'col')), may hold values from -28 to 28
- second_input_proj: float32 [1536, 6144], P('dp', ('row', 'col')), may hold values from 16.384 to 163.84
- state_proj: float32 [1536, 256], P(('dp', 'row', 'col')), may hold values from -0.15625 to 0.15625
- first_state_proj: float32 [1536, 256], P(('dp', 'row', 'col')), may hold values from -28 to 28
- second_state_proj: float32 [1536, 256], P(('dp', 'row', 'col')), may hold values from 16.384 to 163.84
- step_proj: float32 [1536, 48], P(('dp', 'row', 'col')), may hold values from -0.15625 to 0.15625
- first_step_proj: float32 [1536, 48], P(('dp', 'row', 'col')), may hold values from -28 to 28
- second_step_proj: float32 [1536, 48], P(('dp', 'row', 'col')), may hold values from 16.384 to 163.84
- conv_taps: float32 [5, 3328], replicated, may hold values from -0.5 to 0.5
- first_conv_taps: float32 [5, 3328], replicated, may hold values from -28 to 28
- second_conv_taps: float32 [5, 3328], replicated, may hold values from 16.384 to 163.84
- head_coef: float32 [3, 48], replicated, may hold values from -7 to 3
- first_head_coef: float32 [3, 48], replicated, may hold values from -28 to 28
- second_head_coef: float32 [3, 48], replicated, may hold values from 16.384 to 163.84
- gated_gain: float32 [3072], replicated, may hold values from 0.5 to 1.5
- first_gated_gain: float32 [3072], replicated, may hold values from -28 to 28
- second_gated_gain: float32 [3072], replicated, may hold values from 16.384 to 163.84
- output_proj: float32 [3072, 1536], P(('row', 'col'), 'dp'), may hold values from -0.109375 to 0.109375
- first_output_proj: float32 [3072, 1536], P(('row', 'col'), 'dp'), may hold values from -28 to 28
- second_output_proj: float32 [3072, 1536], P(('row', 'col'), 'dp'), may hold values from 16.384 to 163.84
Outputs:
- block_out: bfloat16 [8192, 1536], P(('dp', 'row', 'col'))
- input_grad: float32 [8192, 1536], P(('dp', 'row', 'col'))
- grad_norm_gain: float32 [1536], replicated
- grad_input_proj: float32 [1536, 6144], P('dp', ('row', 'col'))
- grad_state_proj: float32 [1536, 256], P(('dp', 'row', 'col'))
- grad_step_proj: float32 [1536, 48], P(('dp', 'row', 'col'))
- grad_conv_taps: float32 [5, 3328], replicated
- grad_head_coef: float32 [3, 48], replicated
- grad_gated_gain: float32 [3072], replicated
- grad_output_proj: float32 [3072, 1536], P(('row', 'col'), 'dp')
- new_norm_gain: float32 [1536], replicated
- new_first_norm_gain: float32 [1536], replicated
- new_second_norm_gain: float32 [1536], replicated
- new_input_proj: float32 [1536, 6144], P('dp', ('row', 'col'))
- new_first_input_proj: float32 [1536, 6144], P('dp', ('row', 'col'))
- new_second_input_proj: float32 [1536, 6144], P('dp', ('row', 'col'))
- new_state_proj: float32 [1536, 256], P(('dp', 'row', 'col'))
- new_first_state_proj: float32 [1536, 256], P(('dp', 'row', 'col'))
- new_second_state_proj: float32 [1536, 256], P(('dp', 'row', 'col'))
- new_step_proj: float32 [1536, 48], P(('dp', 'row', 'col'))
- new_first_step_proj: float32 [1536, 48], P(('dp', 'row', 'col'))
- new_second_step_proj: float32 [1536, 48], P(('dp', 'row', 'col'))
- new_conv_taps: float32 [5, 3328], replicated
- new_first_conv_taps: float32 [5, 3328], replicated
- new_second_conv_taps: float32 [5, 3328], replicated
- new_head_coef: float32 [3, 48], replicated
- new_first_head_coef: float32 [3, 48], replicated
- new_second_head_coef: float32 [3, 48], replicated
- new_gated_gain: float32 [3072], replicated
- new_first_gated_gain: float32 [3072], replicated
- new_second_gated_gain: float32 [3072], replicated
- new_output_proj: float32 [3072, 1536], P(('row', 'col'), 'dp')
- new_first_output_proj: float32 [3072, 1536], P(('row', 'col'), 'dp')
- new_second_output_proj: float32 [3072, 1536], P(('row', 'col'), 'dp')
All inputs are finite; a program needn't handle non-finite values.
Results may differ from a plain program's by a relative error of at most 0.0034.
The roundings to bfloat16 on the way count: a program that leaves them out, or rounds other values in their place, can miss the bound.
Values may be sent and summed in bfloat16 or wider, within the bound.
No kernel may reach another device: no remote copies, remote signals or barrier semaphores. Data moves between devices by JAX's collectives and lax.ppermute only.
A program may use at most 192 MiB of HBM per device.

v0:
```python
import jax
import jax.numpy as jnp
from jax import lax
from jax.sharding import PartitionSpec as P

SPAN = 256
SEQ_LEN = 1024
ADAM_STEP = 4
PRECISE = lax.Precision.HIGHEST
NORM_EPS = 1e-05
BETA_ONE = 0.9
BETA_TWO = 0.95
ADAM_EPS = 1e-08
MATRIX_RATE = 0.003
VECTOR_RATE = 0.1
WEIGHT_DECAY = 0.1


def causal_conv(values, filters):
    length = values.shape[0]
    padded = jnp.pad(values, ((3, 0), (0, 0)))
    summed = filters[4][None, :] + jnp.zeros_like(values)
    for offset in range(4):
        summed = summed + filters[offset][None, :] * padded[offset : offset + length]
    return summed


def span_scan(values, deltas, rates, key_rows, query_rows):
    length, head_count, head_width = values.shape
    states = key_rows.shape[1]
    blocks = length // SPAN
    values = values.reshape(blocks, SPAN, head_count, head_width)
    deltas = deltas.reshape(blocks, SPAN, head_count)
    key_rows = key_rows.reshape(blocks, SPAN, states)
    query_rows = query_rows.reshape(blocks, SPAN, states)
    log_decay = jnp.cumsum(deltas * rates[None, None, :], axis=1)
    scores = jnp.einsum("kqn,krn->kqr", query_rows, key_rows, precision=PRECISE)
    causal = jnp.arange(SPAN)[:, None] >= jnp.arange(SPAN)[None, :]
    head_decay = jnp.transpose(log_decay, (0, 2, 1))
    head_deltas = jnp.transpose(deltas, (0, 2, 1))
    spread = head_decay[:, :, :, None] - head_decay[:, :, None, :]
    decays = jnp.exp(jnp.where(causal[None, None, :, :], spread, -jnp.inf))
    mixing = scores[:, None, :, :] * decays * head_deltas[:, :, None, :]
    within = jnp.einsum("khqr,krhp->kqhp", mixing, values, precision=PRECISE)
    to_end = jnp.exp(log_decay[:, -1:, :] - log_decay) * deltas
    produced = jnp.einsum("kqn,kqh,kqhp->khnp", key_rows, to_end, values, precision=PRECISE)
    factors = jnp.exp(log_decay[:, -1, :])
    carried = jnp.zeros((head_count, states, head_width), jnp.float32)
    entering = []
    for number in range(blocks):
        entering.append(carried)
        carried = carried * factors[number][:, None, None] + produced[number]
    entering = jnp.stack(entering)
    across = (
        jnp.einsum("kqn,khnp->kqhp", query_rows, entering, precision=PRECISE)
        * jnp.exp(log_decay)[:, :, :, None]
    )
    return (within + across).reshape(length, head_count, head_width)


def mixer_sequence(gate_part, inputs, state_in, step_raw, conv_inner, conv_state, coefs):
    length = inputs.shape[0]
    head_count = coefs.shape[1]
    head_width = inputs.shape[1] // head_count
    state_size = state_in.shape[1] // 2
    conv_out = jax.nn.silu(causal_conv(inputs, conv_inner))
    state_out = jax.nn.silu(causal_conv(state_in, conv_state))
    deltas = jax.nn.softplus(step_raw + coefs[0][None, :])
    rates = -jnp.exp(coefs[1])
    shaped = conv_out.reshape(length, head_count, head_width)
    result = span_scan(shaped, deltas, rates, state_out[:, :state_size], state_out[:, state_size:])
    result = result + coefs[2][None, :, None] * shaped
    return result.reshape(length, head_count * head_width) * jax.nn.silu(gate_part)


def mixer_all(gate_part, inputs, state_in, step_raw, conv_inner, conv_state, coefs):
    seq_count = inputs.shape[0] // SEQ_LEN

    def sequence(pieces):
        return mixer_sequence(
            pieces[0], pieces[1], pieces[2], pieces[3], conv_inner, conv_state, coefs
        )

    gated = lax.map(
        jax.checkpoint(sequence),
        (
            gate_part.reshape(seq_count, SEQ_LEN, -1),
            inputs.reshape(seq_count, SEQ_LEN, -1),
            state_in.reshape(seq_count, SEQ_LEN, -1),
            step_raw.reshape(seq_count, SEQ_LEN, -1),
        ),
    )
    return gated.reshape(inputs.shape[0], -1)


def adamw(weight, gradient, moment_one, moment_two, step_rate, shrink):
    new_one = BETA_ONE * moment_one + (1.0 - BETA_ONE) * gradient
    new_two = BETA_TWO * moment_two + (1.0 - BETA_TWO) * gradient * gradient
    one_hat = new_one / (1.0 - BETA_ONE**ADAM_STEP)
    two_hat = new_two / (1.0 - BETA_TWO**ADAM_STEP)
    updated = weight - step_rate * (one_hat / (jnp.sqrt(two_hat) + ADAM_EPS) + shrink * weight)
    return (updated, new_one, new_two)


def per_device(
    block_in,
    out_grad,
    norm_gain,
    first_norm_gain,
    second_norm_gain,
    input_proj,
    first_input_proj,
    second_input_proj,
    state_proj,
    first_state_proj,
    second_state_proj,
    step_proj,
    first_step_proj,
    second_step_proj,
    conv_taps,
    first_conv_taps,
    second_conv_taps,
    head_coef,
    first_head_coef,
    second_head_coef,
    gated_gain,
    first_gated_gain,
    second_gated_gain,
    output_proj,
    first_output_proj,
    second_output_proj,
):
    groups = lax.axis_size(("row", "col"))
    place = lax.axis_index(("row", "col"))
    tok_dev = block_in.shape[0]
    group_tok = tok_dev * groups
    inner = gated_gain.shape[0]
    inner_dev = inner // groups
    head_total = head_coef.shape[1]
    heads_dev = head_total // groups
    head_width = inner // head_total
    in_local, out_local = (
        lax.all_gather(input_proj.astype(jnp.bfloat16), "dp", axis=0, tiled=True),
        lax.all_gather(output_proj.astype(jnp.bfloat16), "dp", axis=1, tiled=True),
    )
    state_full, step_full = (
        lax.all_gather(state_proj.astype(jnp.bfloat16), ("dp", "row", "col"), axis=0, tiled=True),
        lax.all_gather(step_proj.astype(jnp.bfloat16), ("dp", "row", "col"), axis=0, tiled=True),
    )
    x_float = block_in.astype(jnp.float32)
    inv_rms = lax.rsqrt(jnp.mean(x_float * x_float, axis=1, keepdims=True) + NORM_EPS)
    normed_in = (x_float * inv_rms * norm_gain[None, :]).astype(jnp.bfloat16)
    state_own = jnp.dot(normed_in, state_full, preferred_element_type=jnp.float32).astype(
        jnp.bfloat16
    )
    step_own = jnp.dot(normed_in, step_full, preferred_element_type=jnp.float32).astype(
        jnp.bfloat16
    )
    normed_all, state_all, step_all, cotangent = (
        lax.all_gather(normed_in, ("row", "col"), axis=0, tiled=True),
        lax.all_gather(state_own, ("row", "col"), axis=0, tiled=True),
        lax.all_gather(step_own, ("row", "col"), axis=0, tiled=True),
        lax.all_gather(out_grad, ("row", "col"), axis=0, tiled=True),
    )
    projected = jnp.dot(normed_all, in_local, preferred_element_type=jnp.float32)
    paired = projected.reshape(group_tok, heads_dev, 2, head_width)
    gate_part = paired[:, :, 0, :].reshape(group_tok, inner_dev)
    inputs = paired[:, :, 1, :].reshape(group_tok, inner_dev)
    conv_inner = lax.dynamic_slice_in_dim(conv_taps, place * inner_dev, inner_dev, 1)
    conv_state = conv_taps[:, inner:]
    coefs = lax.dynamic_slice_in_dim(head_coef, place * heads_dev, heads_dev, 1)
    step_local = lax.dynamic_slice_in_dim(step_all, place * heads_dev, heads_dev, 1).astype(
        jnp.float32
    )
    gated, mixer_pull = jax.vjp(
        mixer_all,
        gate_part,
        inputs,
        state_all.astype(jnp.float32),
        step_local,
        conv_inner,
        conv_state,
        coefs,
    )
    squares = lax.psum(jnp.sum(gated * gated, axis=1), ("row", "col"))
    gated_rms = lax.rsqrt(squares / inner + NORM_EPS)[:, None]
    gain_local = lax.dynamic_slice_in_dim(gated_gain, place * inner_dev, inner_dev, 0)
    normed_out = (gated * gated_rms * gain_local[None, :]).astype(jnp.bfloat16)
    rows = normed_out
    mixed = lax.psum_scatter(
        jnp.dot(rows, out_local, preferred_element_type=jnp.float32),
        ("row", "col"),
        scatter_dimension=0,
        tiled=True,
    )
    block_out = (x_float + mixed).astype(jnp.bfloat16)
    grad_out_local = jnp.einsum(
        "tc,td->cd", normed_out, cotangent, preferred_element_type=jnp.float32
    )
    d_normed = jnp.einsum("td,cd->tc", cotangent, out_local, preferred_element_type=jnp.float32)
    gain_part = jnp.sum(d_normed * gated * gated_rms, axis=0)
    scaled = d_normed * gain_local[None, :]
    cross = lax.psum(jnp.sum(scaled * gated, axis=1), ("row", "col"))
    d_gated = gated_rms * scaled - gated * gated_rms**3 * (cross / inner)[:, None]
    d_gate, d_inputs, d_state, d_step, d_conv_inner, d_conv_state, d_coefs = mixer_pull(d_gated)
    d_projected = (
        jnp.stack(
            [
                d_gate.reshape(group_tok, heads_dev, head_width),
                d_inputs.reshape(group_tok, heads_dev, head_width),
            ],
            axis=2,
        )
        .reshape(group_tok, 2 * inner_dev)
        .astype(jnp.bfloat16)
    )
    grad_in_local = jnp.einsum(
        "td,tc->dc", normed_all, d_projected, preferred_element_type=jnp.float32
    )
    rows = d_projected
    d_normed_in = lax.psum_scatter(
        jnp.einsum("tc,dc->td", rows, in_local, preferred_element_type=jnp.float32),
        ("row", "col"),
        scatter_dimension=0,
        tiled=True,
    )
    step_spread = lax.dynamic_update_slice_in_dim(
        jnp.zeros((group_tok, head_total), jnp.float32), d_step, place * heads_dev, 1
    )
    state_back, step_back = (
        lax.psum_scatter(d_state, ("row", "col"), scatter_dimension=0, tiled=True),
        lax.psum_scatter(step_spread, ("row", "col"), scatter_dimension=0, tiled=True),
    )
    state_back = state_back.astype(jnp.bfloat16)
    step_back = step_back.astype(jnp.bfloat16)
    d_normed_in = (
        d_normed_in
        + jnp.einsum("tc,dc->td", state_back, state_full, preferred_element_type=jnp.float32)
        + jnp.einsum("tc,dc->td", step_back, step_full, preferred_element_type=jnp.float32)
    )
    grad_state_part = jnp.einsum(
        "td,tc->dc", normed_in, state_back, preferred_element_type=jnp.float32
    )
    grad_step_part = jnp.einsum(
        "td,tc->dc", normed_in, step_back, preferred_element_type=jnp.float32
    )
    grad_state, grad_step = (
        lax.psum_scatter(grad_state_part, ("dp", "row", "col"), scatter_dimension=0, tiled=True),
        lax.psum_scatter(grad_step_part, ("dp", "row", "col"), scatter_dimension=0, tiled=True),
    )
    grad_input, grad_output = (
        lax.psum_scatter(grad_in_local, "dp", scatter_dimension=0, tiled=True),
        lax.psum_scatter(grad_out_local, "dp", scatter_dimension=1, tiled=True),
    )
    scaled_in = d_normed_in * norm_gain[None, :]
    norm_part = jnp.sum(d_normed_in * x_float * inv_rms, axis=0)
    input_grad = (
        out_grad.astype(jnp.float32)
        + inv_rms * scaled_in
        - x_float * inv_rms**3 * jnp.mean(scaled_in * x_float, axis=1, keepdims=True)
    )
    gated_spread = lax.dynamic_update_slice_in_dim(
        jnp.zeros((inner,), jnp.float32), gain_part, place * inner_dev, 0
    )
    conv_front = lax.dynamic_update_slice_in_dim(
        jnp.zeros((5, inner), jnp.float32), d_conv_inner, place * inner_dev, 1
    )
    conv_spread = jnp.concatenate([conv_front, d_conv_state], axis=1)
    coef_spread = lax.dynamic_update_slice_in_dim(
        jnp.zeros((3, head_total), jnp.float32), d_coefs, place * heads_dev, 1
    )
    grad_norm, grad_gated, grad_conv, grad_coef = lax.psum(
        (norm_part, gated_spread, conv_spread, coef_spread), ("dp", "row", "col")
    )
    n_norm, f_norm, s_norm = adamw(
        norm_gain, grad_norm, first_norm_gain, second_norm_gain, VECTOR_RATE, 0.0
    )
    n_input, f_input, s_input = adamw(
        input_proj, grad_input, first_input_proj, second_input_proj, MATRIX_RATE, WEIGHT_DECAY
    )
    n_state, f_state, s_state = adamw(
        state_proj, grad_state, first_state_proj, second_state_proj, MATRIX_RATE, WEIGHT_DECAY
    )
    n_step, f_step, s_step = adamw(
        step_proj, grad_step, first_step_proj, second_step_proj, MATRIX_RATE, WEIGHT_DECAY
    )
    n_conv, f_conv, s_conv = adamw(
        conv_taps, grad_conv, first_conv_taps, second_conv_taps, VECTOR_RATE, 0.0
    )
    n_head, f_head, s_head = adamw(
        head_coef, grad_coef, first_head_coef, second_head_coef, VECTOR_RATE, 0.0
    )
    n_gated, f_gated, s_gated = adamw(
        gated_gain, grad_gated, first_gated_gain, second_gated_gain, VECTOR_RATE, 0.0
    )
    n_output, f_output, s_output = adamw(
        output_proj, grad_output, first_output_proj, second_output_proj, MATRIX_RATE, WEIGHT_DECAY
    )
    return (
        block_out,
        input_grad,
        grad_norm,
        grad_input,
        grad_state,
        grad_step,
        grad_conv,
        grad_coef,
        grad_gated,
        grad_output,
        n_norm,
        f_norm,
        s_norm,
        n_input,
        f_input,
        s_input,
        n_state,
        f_state,
        s_state,
        n_step,
        f_step,
        s_step,
        n_conv,
        f_conv,
        s_conv,
        n_head,
        f_head,
        s_head,
        n_gated,
        f_gated,
        s_gated,
        n_output,
        f_output,
        s_output,
    )


def solution(mesh):
    return jax.shard_map(
        per_device,
        mesh=mesh,
        in_specs=(
            P(("dp", "row", "col"), None),
            P(("dp", "row", "col"), None),
            P(),
            P(),
            P(),
            P("dp", ("row", "col")),
            P("dp", ("row", "col")),
            P("dp", ("row", "col")),
            P(("dp", "row", "col"), None),
            P(("dp", "row", "col"), None),
            P(("dp", "row", "col"), None),
            P(("dp", "row", "col"), None),
            P(("dp", "row", "col"), None),
            P(("dp", "row", "col"), None),
            P(),
            P(),
            P(),
            P(),
            P(),
            P(),
            P(),
            P(),
            P(),
            P(("row", "col"), "dp"),
            P(("row", "col"), "dp"),
            P(("row", "col"), "dp"),
        ),
        out_specs=(
            P(("dp", "row", "col"), None),
            P(("dp", "row", "col"), None),
            P(),
            P("dp", ("row", "col")),
            P(("dp", "row", "col"), None),
            P(("dp", "row", "col"), None),
            P(),
            P(),
            P(),
            P(("row", "col"), "dp"),
            P(),
            P(),
            P(),
            P("dp", ("row", "col")),
            P("dp", ("row", "col")),
            P("dp", ("row", "col")),
            P(("dp", "row", "col"), None),
            P(("dp", "row", "col"), None),
            P(("dp", "row", "col"), None),
            P(("dp", "row", "col"), None),
            P(("dp", "row", "col"), None),
            P(("dp", "row", "col"), None),
            P(),
            P(),
            P(),
            P(),
            P(),
            P(),
            P(),
            P(),
            P(),
            P(("row", "col"), "dp"),
            P(("row", "col"), "dp"),
            P(("row", "col"), "dp"),
        ),
        check_vma=False,
    )
```

profile of v0, /device:TPU:0, one launch (start us, length us, event | category | flops | bytes accessed | tf_op | source)
XLA Modules:
  0.0 1698.1 jit_solution(3342387534222917837)
XLA Ops:
  10.1 77.2 %all_gather.26 = bf16[1536,256]{1,0:T(8,128)(2,1)S(1)} all-gather(bf16[48,256]{1,0:T(8,128)(2,1)S(1)} %convert_element_type.58), channel_id=1, replica_groups=mesh['dp'=4,'row'=2,'col'=4] {'dp','row','col'}, dimensions={0}, use_global_device_ids=true | all-gather | bytes 811008 | tf_op jit(solution)/shard_map/all_gather | solution.py:147
  95.0 68.2 %all_gather.28 = bf16[1536,48]{1,0:T(8,128)(2,1)S(1)} all-gather(bf16[48,48]{1,0:T(8,128)(2,1)S(1)} %convert_element_type.60), channel_id=1, replica_groups=mesh['dp'=4,'row'=2,'col'=4] {'dp','row','col'}, dimensions={0}, use_global_device_ids=true | all-gather | bytes 152064 | tf_op jit(solution)/shard_map/all_gather | solution.py:148
  164.0 32.7 %all_gather.29 = bf16[2048,48]{0,1:T(8,128)(2,1)S(1)} all-gather(bf16[256,48]{0,1:T(8,128)(2,1)S(1)} %convolution_convert_fusion.1), channel_id=1, replica_groups=mesh['dp'=4,'row'=2,'col'=4] {'row','col'}, dimensions={0}, use_global_device_ids=true | all-gather | bytes 221184 | tf_op jit(solution)/shard_map/all_gather | solution.py:162
  202.5 55.3 %all-gather.6.cloned.1.call-done = bf16[2048,1536]{1,0:T(8,128)(2,1)} async-done(((bf16[256,1536]{1,0:T(8,128)(2,1)}), bf16[2048,1536]{1,0:T(8,128)(2,1)}) %all-gather.6.cloned.1.call-update) | async-done | bytes 6291472 | tf_op jit(solution)/shard_map/all_gather | solution.py:160
  257.7 8.1 fusion.182
  283.0 75.7 %while.43 = (s32[]{:T(128)}, f32[2,1024,384]{1,2,0:T(8,128)}, f32[1,384]{1,0:T(1,128)S(1)}, f32[2,1024,384]{1,2,0:T(8,128)}, f32[1,384]{1,0:T(1,128)S(1)}, /*ind...) while((s32[]{:T(128)}, f32[2,1024,384]{1,2,0:T(8,128)}, ...), condition=%wide.region_4.5_spmd.clone.clone, body=%wide.region_1.4_spmd.clone.sunk.clone | while | flops 2843105280 | bytes 111481648 | solution.py:84
  283.6 7.2 reduce-window.84
  321.3 7.2 reduce-window.84
  362.7 19.9 %psum.42 = f32[2048]{0:T(1024)S(1)} all-reduce(f32[2048]{0:T(1024)S(1)} %bitcast.754), channel_id=1, replica_groups=mesh['dp'=4,'row'=2,'col'=4] {'row','col'}, use_global_device_ids=true, to_apply=%region_6.7 | all-reduce | flops 2048 | bytes 16384 | tf_op jit(solution)/shard_map/psum | solution.py:185
  382.7 10.2 fusion.138
  392.9 18.0 %psum.43 = f32[2048]{0:T(1024)S(1)} all-reduce(f32[2048]{0:T(1024)S(1)} %get-tuple-element.979), channel_id=1, replica_groups=mesh['dp'=4,'row'=2,'col'=4] {'row','col'}, use_global_device_ids=true, to_apply=%region_9.10 | all-reduce | flops 2048 | bytes 16384 | tf_op jit(solution)/shard_map/psum | solution.py:203
  417.3 292.8 %while.44 = (s32[]{:T(128)}, f32[5,384]{1,0:T(8,128)}, f32[5,256]{1,0:T(8,128)}, f32[3,6]{1,0:T(4,128)}, bf16[2,1024,384]{1,2,0:T(8,128)(2,1)}, /*index=5*/bf16[...) while((s32[]{:T(128)}, f32[5,384]{1,0:T(8,128)}, ...), condition=%wide.region_38.39_spmd.clone.clone, body=%wide.region_10.38_spmd.clone.sunk.clone | while | flops 8532760576 | bytes 316975616 | solution.py:84
  429.6 7.2 reduce-window.87
  488.1 8.8 bitcast_add_fusion.16
  496.9 9.6 fusion.380
  511.5 30.6 %reduce-window.88 = f32[4,6,2,128]{3,2,1,0:T(2,128)S(1)} reduce-window(f32[4,6,2,128]{3,2,1,0:T(2,128)S(1)} %reshape.763, f32[]{:T(128)} %constant.263.clone.1..sunk.3), window={size=1x1x1x128 pad=0_0x0_0x0_0x0_127}, to_apply=%region_33.33 | reduce-window | flops 780288 | bytes 49156 | tf_op jit(solution)/shard_map/reduce-window.36
  572.0 7.2 reduce-window.87
  630.6 9.0 bitcast_add_fusion.16
  639.5 9.6 fusion.380
  654.1 30.3 %reduce-window.88 = f32[4,6,2,128]{3,2,1,0:T(2,128)S(1)} reduce-window(f32[4,6,2,128]{3,2,1,0:T(2,128)S(1)} %reshape.763, f32[]{:T(128)} %constant.263.clone.1..sunk.3), window={size=1x1x1x128 pad=0_0x0_0x0_0x0_127}, to_apply=%region_33.33 | reduce-window | flops 780288 | bytes 49156 | tf_op jit(solution)/shard_map/reduce-window.36
  713.8 61.1 %reduce-scatter.15.cloned.1.call-done = f32[256,48]{0,1:T(8,128)} async-done(((f32[2048,48]{0,1:T(8,128)}), f32[256,48]{0,1:T(8,128)}) %reduce-scatter.15.cloned.1.call-update) | async-done | bytes 49168 | tf_op jit(solution)/shard_map/reduce_scatter | solution.py:232
  784.0 62.0 %reduce-scatter.13.cloned.1.call-done = f32[256,256]{1,0:T(8,128)} async-done(((f32[2048,256]{1,0:T(8,128)}), f32[256,256]{1,0:T(8,128)}) %reduce-scatter.13.cloned.1.call-update) | async-done | bytes 262160 | tf_op jit(solution)/shard_map/reduce_scatter | solution.py:231
  869.0 8.8 fusion.185
  877.8 10.4 fusion.184
  896.9 76.9 %all-reduce.38.cloned.1.call-done = f32[5,3328]{1,0:T(8,128)} async-done(((f32[5,3328]{1,0:T(8,128)}), f32[5,3328]{1,0:T(8,128)}) %all-reduce.38.cloned.1.call-update) | async-done | bytes 66576 | tf_op jit(solution)/shard_map/psum | solution.py:272
  975.5 101.2 %reduce-scatter.21.cloned.1.call-done = f32[48,48]{1,0:T(8,128)} async-done(((f32[1536,48]{1,0:T(8,128)}), f32[48,48]{1,0:T(8,128)}) %reduce-scatter.21.cloned.1.call-update) | async-done | bytes 9232 | tf_op jit(solution)/shard_map/reduce_scatter | solution.py:249
  1078.0 33.4 %reduce-scatter.23.cloned.1.call-done = f32[384,384]{1,0:T(8,128)} async-done(((f32[384,1536]{1,0:T(8,128)}), f32[384,384]{1,0:T(8,128)}) %reduce-scatter.23.cloned.1.call-update) | async-done | bytes 589840 | tf_op jit(solution)/shard_map/reduce_scatter | solution.py:253
  1114.0 101.3 %reduce-scatter.19.cloned.1.call-done = f32[48,256]{1,0:T(8,128)} async-done(((f32[1536,256]{1,0:T(8,128)}), f32[48,256]{1,0:T(8,128)}) %reduce-scatter.19.cloned.1.call-update) | async-done | bytes 49168 | tf_op jit(solution)/shard_map/reduce_scatter | solution.py:248
  1216.7 48.5 %reduce-scatter.17.cloned.1.call-done = f32[384,768]{1,0:T(8,128)} async-done(((f32[1536,768]{1,0:T(8,128)}), f32[384,768]{1,0:T(8,128)}) %reduce-scatter.17.cloned.1.call-update) | async-done | bytes 1179664 | tf_op jit(solution)/shard_map/reduce_scatter | solution.py:252
  1269.6 206.7 %reduce-scatter.11.cloned.1.call-done = f32[256,1536]{1,0:T(8,128)} async-done(((f32[2048,1536]{1,0:T(8,128)}), f32[256,1536]{1,0:T(8,128)}) %reduce-scatter.11.cloned.1.call-update) | async-done | bytes 1572880 | tf_op jit(solution)/shard_map/reduce_scatter | solution.py:221
  1479.5 43.5 %all-reduce.35 = (f32[1536]{0:T(1024)S(1)}, f32[3,48]{1,0:T(4,128)S(1)}, f32[3072]{0:T(1024)S(1)}) all-reduce(f32[1536]{0:T(1024)S(1)} %get-tuple-element.980, f32[3,48]{1,0:T(4,128)} %copy-done.151, f32[3072]{0:T(1024)} %copy-done.141), channel_id=1, replica_groups=mesh['dp'=4,'row'=2,'col'=4] {'dp','row','col'}, use_global_device_ids=true, to_apply=%region_44.45 | all-reduce | flops 4752 | bytes 38016 | tf_op jit(solution)/shard_map/psum | solution.py:272
  1527.7 159.6 %reduce-scatter.9.cloned.1.call-done = f32[256,1536]{1,0:T(8,128)} async-done(((f32[2048,1536]{1,0:T(8,128)}), f32[256,1536]{1,0:T(8,128)}) %reduce-scatter.9.cloned.1.call-update) | async-done | bytes 1572880 | tf_op jit(solution)/shard_map/reduce_scatter | solution.py:190
  (885 shorter events, 341.6 us)
Async XLA Ops:
  7.2 192.5 %all-gather.10.cloned.1.call-start = ((), (), s32[]{:S(2)}) async-start(), calls=%async_computation.10 | async-start | bytes 1179648 | tf_op jit(solution)/shard_map/all_gather | solution.py:161
  88.7 113.8 %all-gather.8.cloned.1.call-start = ((), (), s32[]{:S(2)}) async-start(), calls=%async_computation.9 | async-start | bytes 2949120 | tf_op jit(solution)/shard_map/all_gather | solution.py:143
  90.1 167.6 %all-gather.6.cloned.1.call-start = ((), (), s32[]{:S(2)}) async-start(), calls=%async_computation.8 | async-start | bytes 7077888 | tf_op jit(solution)/shard_map/all_gather | solution.py:160
  90.8 291.8 %all-gather.12.cloned.1.call-start = ((), (), s32[]{:S(2)}) async-start(), calls=%async_computation.11 | async-start | bytes 1474560 | tf_op jit(solution)/shard_map/all_gather | solution.py:144
  91.7 291.0 %all-gather.14.cloned.1.call-start = ((), (), s32[]{:S(2)}) async-start(), calls=%async_computation.13 | async-start | bytes 7077888 | tf_op jit(solution)/shard_map/all_gather | solution.py:163
  92.3 682.6 %reduce-scatter.15.cloned.1.call-start = ((), (), s32[]{:S(2)}) async-start(), calls=%async_computation.16 | async-start | bytes 442368 | tf_op jit(solution)/shard_map/reduce_scatter | solution.py:232
  94.1 171.7 %copy-start.45 = (bf16[2,1024,384]{1,2,0:T(8,128)(2,1)}, bf16[2,1024,384]{1,2,0:T(8,128)(2,1)S(1)}, u32[]{:S(2)}) copy-start(bf16[2,1024,384]{1,2,0:T(8,128)(2,1)S(1)} %fusion.176) | copy-start | bytes 4718596
  712.2 133.8 %reduce-scatter.13.cloned.1.call-start = ((), (), s32[]{:S(2)}) async-start(), calls=%async_computation.15 | async-start | bytes 2359296 | tf_op jit(solution)/shard_map/reduce_scatter | solution.py:231
  713.0 260.8 %all-reduce.38.cloned.1.call-start = ((), (), s32[]{:S(2)}) async-start(), calls=%async_computation.20 | async-start | bytes 212992 | tf_op jit(solution)/shard_map/psum | solution.py:272
  713.8 362.9 %reduce-scatter.21.cloned.1.call-start = ((), (), s32[]{:S(2)}) async-start(), calls=%async_computation.19 | async-start | bytes 811008 | tf_op jit(solution)/shard_map/reduce_scatter | solution.py:249
  777.0 334.4 %reduce-scatter.23.cloned.1.call-start = ((), (), s32[]{:S(2)}) async-start(), calls=%async_computation.21 | async-start | bytes 2949120 | tf_op jit(solution)/shard_map/reduce_scatter | solution.py:253
  783.9 431.3 %reduce-scatter.19.cloned.1.call-start = ((), (), s32[]{:S(2)}) async-start(), calls=%async_computation.18 | async-start | bytes 1622016 | tf_op jit(solution)/shard_map/reduce_scatter | solution.py:248
  848.5 416.7 %reduce-scatter.17.cloned.1.call-start = ((), (), s32[]{:S(2)}) async-start(), calls=%async_computation.17 | async-start | bytes 5898240 | tf_op jit(solution)/shard_map/reduce_scatter | solution.py:252
  877.8 598.6 %reduce-scatter.11.cloned.1.call-start = ((), (), s32[]{:S(2)}) async-start(), calls=%async_computation.14 | async-start | bytes 14155776 | tf_op jit(solution)/shard_map/reduce_scatter | solution.py:221
  888.2 799.1 %reduce-scatter.9.cloned.1.call-start = ((), (), s32[]{:S(2)}) async-start(), calls=%async_computation.12 | async-start | bytes 14155776 | tf_op jit(solution)/shard_map/reduce_scatter | solution.py:190
  895.9 180.8 %copy-start.134 = (f32[48,48]{1,0:T(8,128)S(1)}, f32[48,48]{1,0:T(8,128)}, u32[]{:S(2)}) copy-start(f32[48,48]{1,0:T(8,128)} %param.41) | copy-start | bytes 27652
  895.9 180.8 %copy-start.144 = (f32[48,48]{1,0:T(8,128)S(1)}, f32[48,48]{1,0:T(8,128)}, u32[]{:S(2)}) copy-start(f32[48,48]{1,0:T(8,128)} %param.42) | copy-start | bytes 27652
  895.9 180.8 %copy-start.145 = (f32[48,48]{1,0:T(8,128)S(1)}, f32[48,48]{1,0:T(8,128)}, u32[]{:S(2)}) copy-start(f32[48,48]{1,0:T(8,128)} %param.43) | copy-start | bytes 27652
  895.9 215.6 %copy-start.77 = (f32[384,384]{1,0:T(8,128)S(1)}, f32[384,384]{1,0:T(8,128)}, u32[]{:S(2)}) copy-start(f32[384,384]{1,0:T(8,128)} %param.53) | copy-start | bytes 1769476
  895.9 215.6 %copy-start.87 = (f32[384,384]{1,0:T(8,128)S(1)}, f32[384,384]{1,0:T(8,128)}, u32[]{:S(2)}) copy-start(f32[384,384]{1,0:T(8,128)} %param.54) | copy-start | bytes 1769476
  895.9 215.6 %copy-start.88 = (f32[384,384]{1,0:T(8,128)S(1)}, f32[384,384]{1,0:T(8,128)}, u32[]{:S(2)}) copy-start(f32[384,384]{1,0:T(8,128)} %param.55) | copy-start | bytes 1769476
  896.7 217.3 %copy-start.141 = (f32[3072]{0:T(1024)}, f32[3072]{0:T(1024)S(1)}, u32[]{:S(2)}) copy-start(f32[3072]{0:T(1024)S(1)} %dynamic_update_slice.62) | copy-start | bytes 36868
  896.8 179.8 %copy-start.151 = (f32[3,48]{1,0:T(4,128)}, f32[3,48]{1,0:T(4,128)S(1)}, u32[]{:S(2)}) copy-start(f32[3,48]{1,0:T(4,128)S(1)} %dynamic_update_slice.61) | copy-start | bytes 1732
  1078.0 187.2 %copy-start.67 = (f32[384,768]{1,0:T(8,128)S(1)}, f32[384,768]{1,0:T(8,128)}, u32[]{:S(2)}) copy-start(f32[384,768]{1,0:T(8,128)} %param.35) | copy-start | bytes 3538948
  1216.7 259.6 %copy-start.63 = (bf16[1536,256]{1,0:T(8,128)(2,1)S(1)}, bf16[1536,256]{1,0:T(8,128)(2,1)}, u32[]{:S(2)}) copy-start(bf16[1536,256]{1,0:T(8,128)(2,1)} %copy-done.62) | copy-start | bytes 2359300
  1216.7 259.6 %copy-start.84 = (f32[256,256]{1,0:T(8,128)S(1)}, f32[256,256]{1,0:T(8,128)}, u32[]{:S(2)}) copy-start(f32[256,256]{1,0:T(8,128)} %reduce-scatter.13.cloned.1.call-done) | copy-start | bytes 786436
  1269.6 208.6 %copy-start.52 = (bf16[256,1536]{1,0:T(8,128)(2,1)S(1)}, bf16[256,1536]{1,0:T(8,128)(2,1)}, u32[]{:S(2)}) copy-start(bf16[256,1536]{1,0:T(8,128)(2,1)} %param.30) | copy-start | bytes 2359300
  1269.6 208.6 %copy-start.69 = (bf16[1536,48]{1,0:T(8,128)(2,1)S(1)}, bf16[1536,48]{1,0:T(8,128)(2,1)}, u32[]{:S(2)}) copy-start(bf16[1536,48]{1,0:T(8,128)(2,1)} %copy-done.68) | copy-start | bytes 442372
  1269.6 208.6 %copy-start.124 = (f32[1536]{0:T(1024)S(1)}, f32[1536]{0:T(1024)}, u32[]{:S(2)}) copy-start(f32[1536]{0:T(1024)} %param.32) | copy-start | bytes 18436
  1478.2 209.1 %copy-start.72 = (bf16[256,1536]{1,0:T(8,128)(2,1)S(1)}, bf16[256,1536]{1,0:T(8,128)(2,1)}, u32[]{:S(2)}) copy-start(bf16[256,1536]{1,0:T(8,128)(2,1)} %param.31) | copy-start | bytes 2359300
  1523.0 167.8 %copy-start.149 = (f32[1536]{0:T(1024)}, f32[1536]{0:T(1024)S(1)}, u32[]{:S(2)}) copy-start(f32[1536]{0:T(1024)S(1)} %get-tuple-element.1830) | copy-start | bytes 18436
  1523.0 167.8 %copy-start.152 = (f32[3,48]{1,0:T(4,128)}, f32[3,48]{1,0:T(4,128)S(1)}, u32[]{:S(2)}) copy-start(f32[3,48]{1,0:T(4,128)S(1)} %get-tuple-element.1835) | copy-start | bytes 1732
  (240 other events, 2083.1 us)
Sparse Core Ops, SparseCore 0:
  88.8 38.3 all-gather.9
  129.3 23.3 all-gather.7
  155.3 102.3 all-gather.5
  259.7 15.6 all-gather.11
  277.3 99.5 all-gather.13
  712.3 62.5 reduce-scatter.14
  778.4 67.5 reduce-scatter.12
  852.1 121.6 all-reduce.37
  979.5 97.1 reduce-scatter.20
  1079.6 31.8 reduce-scatter.22
  1117.3 97.9 reduce-scatter.18
  1218.2 47.0 reduce-scatter.16
  1268.9 207.4 reduce-scatter.10
  1479.8 207.4 reduce-scatter.8
where the time goes:
time: 1710 us; the launch traced here: 1700 us
  waiting for transfers between devices  908 us (53%)
  blocking collectives  260 us (15%)
  other arithmetic  195 us (11%)
  matrix products  170 us (10%)
  local copies, waits for them, and re-layouts  138 us (8%)
    reduce_scatter x1, waiting for transfers between devices, per_device(): lax.psum_scatter(jnp.einsum('tc,dc->td', rows, in_local, preferred_elemen...  207 us
    reduce_scatter x1, waiting for transfers between devices, per_device(): lax.psum_scatter(jnp.dot(rows, out_local, preferred_element_type=jnp.floa...  160 us
    reduce_scatter x1, waiting for transfers between devices, per_device(): lax.psum_scatter(grad_state_part, ('dp', 'row', 'col'), scatter_dimension...  101 us
    reduce_scatter x1, waiting for transfers between devices, per_device(): lax.psum_scatter(grad_step_part, ('dp', 'row', 'col'), scatter_dimension=...  101 us
    another operation x25, other arithmetic  91 us
    all_gather x1, blocking collectives, per_device(): lax.all_gather(state_proj.astype(jnp.bfloat16), ('dp', 'row', 'col'), axi...  77.2 us
    psum x1, waiting for transfers between devices, per_device(): lax.psum((norm_part, gated_spread, conv_spread, coef_spread), ('dp', 'row...  76.9 us
    all_gather x1, blocking collectives, per_device(): lax.all_gather(step_proj.astype(jnp.bfloat16), ('dp', 'row', 'col'), axis...  68.2 us
  transfers between devices with their start and end apart: 14, of which 10 were waited for; matrix products, arithmetic and copies ran while one was open for 10% of the time, Pallas kernels for 0%

commit v1 on v0

--- a/solution.py
+++ b/solution.py
@@ -14,6 +14,21 @@
 MATRIX_RATE = 0.003
 VECTOR_RATE = 0.1
 WEIGHT_DECAY = 0.1
+
+
+def spots_compute(mesh_ax, payload):
+    r_now = lax.psum(1, axis_name=mesh_ax)
+    r2, outer, arr_now = (r_now, lax.axis_index(mesh_ax), payload.shape[0])
+    v1, big = (payload, 1)
+    while big < r2:
+        by_place = []
+        for j in [*range(r2)]:
+            by_place.append((j, (j - big) % r2))
+        long_array = lax.ppermute(v1, axis_name=mesh_ax, perm=by_place)
+        v1 = jnp.concatenate([v1, long_array], 0)
+        big = 2 * big
+    oldest = jnp.roll(v1, outer * arr_now, 0)
+    return oldest
 
 
 def causal_conv(values, filters):
@@ -157,7 +172,7 @@
         jnp.bfloat16
     )
     normed_all, state_all, step_all, cotangent = (
-        lax.all_gather(normed_in, ("row", "col"), axis=0, tiled=True),
+        spots_compute(("row", "col"), normed_in),
         lax.all_gather(state_own, ("row", "col"), axis=0, tiled=True),
         lax.all_gather(step_own, ("row", "col"), axis=0, tiled=True),
         lax.all_gather(out_grad, ("row", "col"), axis=0, tiled=True),

time: 1710 us -> 1770 us (1.035)
  waiting for transfers between devices: 908 us -> 939 us
    ppermute x0 -> x3, waiting for transfers between devices: none -> 87.1 us  [spots_compute(): long_array = lax.ppermute(v1, axis_name=mesh_ax, perm=by_place)]
    all_gather x1 -> x0, waiting for transfers between devices: 55.3 us -> none  [per_device(): lax.all_gather(normed_in, ('row', 'col'), axis=0, tiled=True)]
  transfers between devices with their start and end apart: 14 -> 16, of which waited for: 10 -> 11; matrix products, arithmetic and copies ran while one was open for 10% -> 11% of each run, Pallas kernels for 0% -> 0%
where the time goes in v1:
time: 1770 us; the launch traced here: 1760 us
  waiting for transfers between devices  939 us (53%)
  blocking collectives  265 us (15%)
  other arithmetic  199 us (11%)
  matrix products  170 us (10%)
  local copies, waits for them, and re-layouts  151 us (9%)
    reduce_scatter x1, waiting for transfers between devices, per_device(): lax.psum_scatter(jnp.einsum('tc,dc->td', rows, in_local, preferred_elemen...  207 us
    reduce_scatter x1, waiting for transfers between devices, per_device(): lax.psum_scatter(jnp.dot(rows, out_local, preferred_element_type=jnp.floa...  160 us
    reduce_scatter x1, waiting for transfers between devices, per_device(): lax.psum_scatter(grad_step_part, ('dp', 'row', 'col'), scatter_dimension=...  102 us
    reduce_scatter x1, waiting for transfers between devices, per_device(): lax.psum_scatter(grad_state_part, ('dp', 'row', 'col'), scatter_dimension...  101 us
    another operation x25, other arithmetic  91 us
    ppermute x3, waiting for transfers between devices, spots_compute(): long_array = lax.ppermute(v1, axis_name=mesh_ax, perm=by_place)  87.1 us
    all_gather x1, blocking collectives, per_device(): lax.all_gather(state_proj.astype(jnp.bfloat16), ('dp', 'row', 'col'), axi...  77.3 us
    psum x1, waiting for transfers between devices, per_device(): lax.psum((norm_part, gated_spread, conv_spread, coef_spread), ('dp', 'row...  77.2 us
  transfers between devices with their start and end apart: 16, of which 11 were waited for; matrix products, arithmetic and copies ran while one was open for 11% of the time, Pallas kernels for 0%

profile of v1, /device:TPU:0, one launch (start us, length us, event | category | flops | bytes accessed | tf_op | source)
XLA Modules:
  0.0 1762.9 jit_solution(6667814103692262516)
XLA Ops:
  10.1 77.3 %all_gather.22 = bf16[1536,256]{1,0:T(8,128)(2,1)S(1)} all-gather(bf16[48,256]{1,0:T(8,128)(2,1)S(1)} %convert_element_type.58), channel_id=1, replica_groups=mesh['dp'=4,'row'=2,'col'=4] {'dp','row','col'}, dimensions={0}, use_global_device_ids=true | all-gather | bytes 811008 | tf_op jit(solution)/shard_map/all_gather | solution.py:162
  90.7 20.7 %collective-permute-done = bf16[256,1536]{1,0:T(8,128)(2,1)S(1)} collective-permute-done((bf16[256,1536]{1,0:T(8,128)(2,1)S(1)}, bf16[256,1536]{1,0:T(8,128)(2,1)S(1)}, u32[]{:S(2)}, u32[]{:S(2)}) %collective-permute-start) | collective-permute-done | bytes 786464 | tf_op jit(solution)/shard_map/ppermute | solution.py:27
  114.6 66.5 %collective-permute-done.1 = bf16[512,1536]{1,0:T(8,128)(2,1)S(1)} collective-permute-done((bf16[512,1536]{1,0:T(8,128)(2,1)}, bf16[512,1536]{1,0:T(8,128)(2,1)S(1)}, u32[]{:S(2)}, u32[]{:S(2)}) %collective-permute-start.1) | collective-permute-done | bytes 1572896 | tf_op jit(solution)/shard_map/ppermute | solution.py:27
  182.9 10.3 collective-permute-start.2
  196.5 73.6 %all_gather.24 = bf16[1536,48]{1,0:T(8,128)(2,1)S(1)} all-gather(bf16[48,48]{1,0:T(8,128)(2,1)S(1)} %convert_element_type.60), channel_id=1, replica_groups=mesh['dp'=4,'row'=2,'col'=4] {'dp','row','col'}, dimensions={0}, use_global_device_ids=true | all-gather | bytes 152064 | tf_op jit(solution)/shard_map/all_gather | solution.py:163
  271.2 32.7 %all_gather.25 = bf16[2048,48]{0,1:T(8,128)(2,1)S(1)} all-gather(bf16[256,48]{0,1:T(8,128)(2,1)S(1)} %convolution_convert_fusion.1), channel_id=1, replica_groups=mesh['dp'=4,'row'=2,'col'=4] {'row','col'}, dimensions={0}, use_global_device_ids=true | all-gather | bytes 221184 | tf_op jit(solution)/shard_map/all_gather | solution.py:177
  323.2 8.1 fusion.134
  348.5 75.6 %while.43 = (s32[]{:T(128)}, f32[2,1024,384]{1,2,0:T(8,128)}, f32[1,384]{1,0:T(1,128)S(1)}, f32[2,1024,384]{1,2,0:T(8,128)}, f32[1,384]{1,0:T(1,128)S(1)}, /*ind...) while((s32[]{:T(128)}, f32[2,1024,384]{1,2,0:T(8,128)}, ...), condition=%wide.region_4.5_spmd.clone.clone, body=%wide.region_1.4_spmd.clone.sunk.clone | while | flops 2843105280 | bytes 111481648 | solution.py:99
  349.1 7.2 reduce-window.84
  428.1 17.7 %psum.42 = f32[2048]{0:T(1024)S(1)} all-reduce(f32[2048]{0:T(1024)S(1)} %bitcast.752), channel_id=1, replica_groups=mesh['dp'=4,'row'=2,'col'=4] {'row','col'}, use_global_device_ids=true, to_apply=%region_6.7 | all-reduce | flops 2048 | bytes 16384 | tf_op jit(solution)/shard_map/psum | solution.py:200
  445.9 10.1 fusion.142
  456.0 20.2 %psum.43 = f32[2048]{0:T(1024)S(1)} all-reduce(f32[2048]{0:T(1024)S(1)} %get-tuple-element.979), channel_id=1, replica_groups=mesh['dp'=4,'row'=2,'col'=4] {'row','col'}, use_global_device_ids=true, to_apply=%region_9.10 | all-reduce | flops 2048 | bytes 16384 | tf_op jit(solution)/shard_map/psum | solution.py:218
  482.4 292.7 %while.44 = (s32[]{:T(128)}, f32[5,384]{1,0:T(8,128)}, f32[5,256]{1,0:T(8,128)}, f32[3,6]{1,0:T(4,128)}, bf16[2,1024,384]{1,2,0:T(8,128)(2,1)}, /*index=5*/bf16[...) while((s32[]{:T(128)}, f32[5,384]{1,0:T(8,128)}, ...), condition=%wide.region_38.39_spmd.clone.clone, body=%wide.region_10.38_spmd.clone.sunk.clone | while | flops 8532760576 | bytes 316975616 | solution.py:99
  553.2 8.8 bitcast_add_fusion.16
  562.0 9.6 fusion.383
  576.5 30.6 %reduce-window.88 = f32[4,6,2,128]{3,2,1,0:T(2,128)S(1)} reduce-window(f32[4,6,2,128]{3,2,1,0:T(2,128)S(1)} %reshape.763, f32[]{:T(128)} %constant.282.clone.1..sunk.3), window={size=1x1x1x128 pad=0_0x0_0x0_0x0_127}, to_apply=%region_33.33 | reduce-window | flops 780288 | bytes 49156 | tf_op jit(solution)/shard_map/reduce-window.36
  637.0 7.2 reduce-window.87
  695.6 9.0 bitcast_add_fusion.16
  704.6 9.6 fusion.383
  719.1 30.3 %reduce-window.88 = f32[4,6,2,128]{3,2,1,0:T(2,128)S(1)} reduce-window(f32[4,6,2,128]{3,2,1,0:T(2,128)S(1)} %reshape.763, f32[]{:T(128)} %constant.282.clone.1..sunk.3), window={size=1x1x1x128 pad=0_0x0_0x0_0x0_127}, to_apply=%region_33.33 | reduce-window | flops 780288 | bytes 49156 | tf_op jit(solution)/shard_map/reduce-window.36
  778.6 60.5 %reduce-scatter.15.cloned.1.call-done = f32[256,48]{0,1:T(8,128)} async-done(((f32[2048,48]{0,1:T(8,128)}), f32[256,48]{0,1:T(8,128)}) %reduce-scatter.15.cloned.1.call-update) | async-done | bytes 49168 | tf_op jit(solution)/shard_map/reduce_scatter | solution.py:247
  848.3 61.9 %reduce-scatter.13.cloned.1.call-done = f32[256,256]{1,0:T(8,128)} async-done(((f32[2048,256]{1,0:T(8,128)}), f32[256,256]{1,0:T(8,128)}) %reduce-scatter.13.cloned.1.call-update) | async-done | bytes 262160 | tf_op jit(solution)/shard_map/reduce_scatter | solution.py:246
  932.9 8.7 fusion.132
  941.7 10.4 fusion.190
  960.7 77.2 %all-reduce.38.cloned.1.call-done = f32[5,3328]{1,0:T(8,128)} async-done(((f32[5,3328]{1,0:T(8,128)}), f32[5,3328]{1,0:T(8,128)}) %all-reduce.38.cloned.1.call-update) | async-done | bytes 66576 | tf_op jit(solution)/shard_map/psum | solution.py:287
  1039.6 101.7 %reduce-scatter.21.cloned.1.call-done = f32[48,48]{1,0:T(8,128)} async-done(((f32[1536,48]{1,0:T(8,128)}), f32[48,48]{1,0:T(8,128)}) %reduce-scatter.21.cloned.1.call-update) | async-done | bytes 9232 | tf_op jit(solution)/shard_map/reduce_scatter | solution.py:264
  1142.7 33.6 %reduce-scatter.23.cloned.1.call-done = f32[384,384]{1,0:T(8,128)} async-done(((f32[384,1536]{1,0:T(8,128)}), f32[384,384]{1,0:T(8,128)}) %reduce-scatter.23.cloned.1.call-update) | async-done | bytes 589840 | tf_op jit(solution)/shard_map/reduce_scatter | solution.py:268
  1178.8 101.1 %reduce-scatter.19.cloned.1.call-done = f32[48,256]{1,0:T(8,128)} async-done(((f32[1536,256]{1,0:T(8,128)}), f32[48,256]{1,0:T(8,128)}) %reduce-scatter.19.cloned.1.call-update) | async-done | bytes 49168 | tf_op jit(solution)/shard_map/reduce_scatter | solution.py:263
  1281.4 48.7 %reduce-scatter.17.cloned.1.call-done = f32[384,768]{1,0:T(8,128)} async-done(((f32[1536,768]{1,0:T(8,128)}), f32[384,768]{1,0:T(8,128)}) %reduce-scatter.17.cloned.1.call-update) | async-done | bytes 1179664 | tf_op jit(solution)/shard_map/reduce_scatter | solution.py:267
  1334.5 206.6 %reduce-scatter.11.cloned.1.call-done = f32[256,1536]{1,0:T(8,128)} async-done(((f32[2048,1536]{1,0:T(8,128)}), f32[256,1536]{1,0:T(8,128)}) %reduce-scatter.11.cloned.1.call-update) | async-done | bytes 1572880 | tf_op jit(solution)/shard_map/reduce_scatter | solution.py:236
  1544.2 43.4 %all-reduce.35 = (f32[1536]{0:T(1024)S(1)}, f32[3,48]{1,0:T(4,128)S(1)}, f32[3072]{0:T(1024)S(1)}) all-reduce(f32[1536]{0:T(1024)S(1)} %get-tuple-element.980, f32[3,48]{1,0:T(4,128)} %copy-done.150, f32[3072]{0:T(1024)} %copy-done.140), channel_id=1, replica_groups=mesh['dp'=4,'row'=2,'col'=4] {'dp','row','col'}, use_global_device_ids=true, to_apply=%region_44.45 | all-reduce | flops 4752 | bytes 38016 | tf_op jit(solution)/shard_map/psum | solution.py:287
  1592.4 159.7 %reduce-scatter.9.cloned.1.call-done = f32[256,1536]{1,0:T(8,128)} async-done(((f32[2048,1536]{1,0:T(8,128)}), f32[256,1536]{1,0:T(8,128)}) %reduce-scatter.9.cloned.1.call-update) | async-done | bytes 1572880 | tf_op jit(solution)/shard_map/reduce_scatter | solution.py:205
  (895 shorter events, 373.2 us)
Async XLA Ops:
  7.2 301.1 %all-gather.7.cloned.1.call-start = ((), (), s32[]{:S(2)}) async-start(), calls=%async_computation.9 | async-start | bytes 1179648 | tf_op jit(solution)/shard_map/all_gather | solution.py:176
  88.6 227.7 %copy-start.28 = (bf16[256,1536]{1,0:T(8,128)(2,1)}, bf16[256,1536]{1,0:T(8,128)(2,1)S(1)}, u32[]{:S(2)}) copy-start(bf16[256,1536]{1,0:T(8,128)(2,1)S(1)} %get-tuple-element.1099) | copy-start | bytes 2359300
  89.6 233.5 %all-gather.5.cloned.1.call-start = ((), (), s32[]{:S(2)}) async-start(), calls=%async_computation.8 | async-start | bytes 2949120 | tf_op jit(solution)/shard_map/all_gather | solution.py:158
  90.6 355.3 %all-gather.9.cloned.1.call-start = ((), (), s32[]{:S(2)}) async-start(), calls=%async_computation.10 | async-start | bytes 1474560 | tf_op jit(solution)/shard_map/all_gather | solution.py:159
  90.6 20.7 %collective-permute-start = (bf16[256,1536]{1,0:T(8,128)(2,1)S(1)}, bf16[256,1536]{1,0:T(8,128)(2,1)S(1)}, u32[]{:S(2)}, u32[]{:S(2)}) collective-permute-start(bf16[256,1536]{1,0:T(8,128)(2,1)S(1)} %get-tuple-element.1099), channel_id=1, source_target_pairs={{0,7},{1,0},{2,1},{3,2},{4,3},{5,4},{6,5},{7,6},{8,15},{9,8},{10,9... | collective-permute-start | bytes 2359304 | tf_op jit(solution)/shard_map/ppermute | solution.py:27
  112.6 68.4 %collective-permute-start.1 = (bf16[512,1536]{1,0:T(8,128)(2,1)}, bf16[512,1536]{1,0:T(8,128)(2,1)S(1)}, u32[]{:S(2)}, u32[]{:S(2)}) collective-permute-start(bf16[512,1536]{1,0:T(8,128)(2,1)} %pad_maximum_fusion.5), channel_id=1, source_target_pairs={{0,6},{1,7},{2,0},{3,1},{4,2},{5,3},{6,4},{7,5},{8,14},{9,15},{10,... | collective-permute-start | bytes 4718600 | tf_op jit(solution)/shard_map/ppermute | solution.py:27
  114.5 331.3 %all-gather.11.cloned.1.call-start = ((), (), s32[]{:S(2)}) async-start(), calls=%async_computation.12 | async-start | bytes 7077888 | tf_op jit(solution)/shard_map/all_gather | solution.py:178
  182.9 129.5 %collective-permute-start.2 = (bf16[1024,1536]{1,0:T(8,128)(2,1)}, bf16[1024,1536]{1,0:T(8,128)(2,1)}, u32[]{:S(2)}, u32[]{:S(2)}) collective-permute-start(bf16[1024,1536]{1,0:T(8,128)(2,1)} %pad_maximum_fusion.3), channel_id=1, source_target_pairs={{0,4},{1,5},{2,6},{3,7},{4,0},{5,1},{6,2},{7,3},{8,12},{9,13},{10,... | collective-permute-start | bytes 9437192 | tf_op jit(solution)/shard_map/ppermute | solution.py:27
  193.2 646.0 %reduce-scatter.15.cloned.1.call-start = ((), (), s32[]{:S(2)}) async-start(), calls=%async_computation.15 | async-start | bytes 442368 | tf_op jit(solution)/shard_map/reduce_scatter | solution.py:247
  777.2 133.0 %reduce-scatter.13.cloned.1.call-start = ((), (), s32[]{:S(2)}) async-start(), calls=%async_computation.14 | async-start | bytes 2359296 | tf_op jit(solution)/shard_map/reduce_scatter | solution.py:246
  777.8 260.1 %all-reduce.38.cloned.1.call-start = ((), (), s32[]{:S(2)}) async-start(), calls=%async_computation.19 | async-start | bytes 212992 | tf_op jit(solution)/shard_map/psum | solution.py:287
  778.6 362.7 %reduce-scatter.21.cloned.1.call-start = ((), (), s32[]{:S(2)}) async-start(), calls=%async_computation.18 | async-start | bytes 811008 | tf_op jit(solution)/shard_map/reduce_scatter | solution.py:264
  841.3 335.0 %reduce-scatter.23.cloned.1.call-start = ((), (), s32[]{:S(2)}) async-start(), calls=%async_computation.20 | async-start | bytes 2949120 | tf_op jit(solution)/shard_map/reduce_scatter | solution.py:268
  848.2 431.7 %reduce-scatter.19.cloned.1.call-start = ((), (), s32[]{:S(2)}) async-start(), calls=%async_computation.17 | async-start | bytes 1622016 | tf_op jit(solution)/shard_map/reduce_scatter | solution.py:263
  912.7 417.4 %reduce-scatter.17.cloned.1.call-start = ((), (), s32[]{:S(2)}) async-start(), calls=%async_computation.16 | async-start | bytes 5898240 | tf_op jit(solution)/shard_map/reduce_scatter | solution.py:267
  941.7 599.3 %reduce-scatter.11.cloned.1.call-start = ((), (), s32[]{:S(2)}) async-start(), calls=%async_computation.13 | async-start | bytes 14155776 | tf_op jit(solution)/shard_map/reduce_scatter | solution.py:236
  952.1 800.0 %reduce-scatter.9.cloned.1.call-start = ((), (), s32[]{:S(2)}) async-start(), calls=%async_computation.11 | async-start | bytes 14155776 | tf_op jit(solution)/shard_map/reduce_scatter | solution.py:205
  959.7 181.6 %copy-start.133 = (f32[48,48]{1,0:T(8,128)S(1)}, f32[48,48]{1,0:T(8,128)}, u32[]{:S(2)}) copy-start(f32[48,48]{1,0:T(8,128)} %param.41) | copy-start | bytes 27652
  959.7 181.6 %copy-start.143 = (f32[48,48]{1,0:T(8,128)S(1)}, f32[48,48]{1,0:T(8,128)}, u32[]{:S(2)}) copy-start(f32[48,48]{1,0:T(8,128)} %param.42) | copy-start | bytes 27652
  959.7 181.6 %copy-start.144 = (f32[48,48]{1,0:T(8,128)S(1)}, f32[48,48]{1,0:T(8,128)}, u32[]{:S(2)}) copy-start(f32[48,48]{1,0:T(8,128)} %param.43) | copy-start | bytes 27652
  959.7 216.6 %copy-start.76 = (f32[384,384]{1,0:T(8,128)S(1)}, f32[384,384]{1,0:T(8,128)}, u32[]{:S(2)}) copy-start(f32[384,384]{1,0:T(8,128)} %param.53) | copy-start | bytes 1769476
  959.7 216.5 %copy-start.86 = (f32[384,384]{1,0:T(8,128)S(1)}, f32[384,384]{1,0:T(8,128)}, u32[]{:S(2)}) copy-start(f32[384,384]{1,0:T(8,128)} %param.54) | copy-start | bytes 1769476
  959.8 216.5 %copy-start.87 = (f32[384,384]{1,0:T(8,128)S(1)}, f32[384,384]{1,0:T(8,128)}, u32[]{:S(2)}) copy-start(f32[384,384]{1,0:T(8,128)} %param.55) | copy-start | bytes 1769476
  960.5 218.3 %copy-start.140 = (f32[3072]{0:T(1024)}, f32[3072]{0:T(1024)S(1)}, u32[]{:S(2)}) copy-start(f32[3072]{0:T(1024)S(1)} %dynamic_update_slice.62) | copy-start | bytes 36868
  960.7 180.6 %copy-start.150 = (f32[3,48]{1,0:T(4,128)}, f32[3,48]{1,0:T(4,128)S(1)}, u32[]{:S(2)}) copy-start(f32[3,48]{1,0:T(4,128)S(1)} %dynamic_update_slice.61) | copy-start | bytes 1732
  1142.7 187.4 %copy-start.66 = (f32[384,768]{1,0:T(8,128)S(1)}, f32[384,768]{1,0:T(8,128)}, u32[]{:S(2)}) copy-start(f32[384,768]{1,0:T(8,128)} %param.35) | copy-start | bytes 3538948
  1281.4 259.6 %copy-start.62 = (bf16[1536,256]{1,0:T(8,128)(2,1)S(1)}, bf16[1536,256]{1,0:T(8,128)(2,1)}, u32[]{:S(2)}) copy-start(bf16[1536,256]{1,0:T(8,128)(2,1)} %copy-done.61) | copy-start | bytes 2359300
  1281.4 259.6 %copy-start.83 = (f32[256,256]{1,0:T(8,128)S(1)}, f32[256,256]{1,0:T(8,128)}, u32[]{:S(2)}) copy-start(f32[256,256]{1,0:T(8,128)} %reduce-scatter.13.cloned.1.call-done) | copy-start | bytes 786436
  1334.4 208.4 %copy-start.51 = (bf16[256,1536]{1,0:T(8,128)(2,1)S(1)}, bf16[256,1536]{1,0:T(8,128)(2,1)}, u32[]{:S(2)}) copy-start(bf16[256,1536]{1,0:T(8,128)(2,1)} %param.30) | copy-start | bytes 2359300
  1334.4 208.4 %copy-start.68 = (bf16[1536,48]{1,0:T(8,128)(2,1)S(1)}, bf16[1536,48]{1,0:T(8,128)(2,1)}, u32[]{:S(2)}) copy-start(bf16[1536,48]{1,0:T(8,128)(2,1)} %copy-done.67) | copy-start | bytes 442372
  1334.4 208.4 %copy-start.123 = (f32[1536]{0:T(1024)S(1)}, f32[1536]{0:T(1024)}, u32[]{:S(2)}) copy-start(f32[1536]{0:T(1024)} %param.32) | copy-start | bytes 18436
  1542.9 209.2 %copy-start.71 = (bf16[256,1536]{1,0:T(8,128)(2,1)S(1)}, bf16[256,1536]{1,0:T(8,128)(2,1)}, u32[]{:S(2)}) copy-start(bf16[256,1536]{1,0:T(8,128)(2,1)} %param.31) | copy-start | bytes 2359300
  (241 other events, 2550.0 us)
Sparse Core Ops, SparseCore 0:
  89.7 74.9 all-gather.6
  166.9 41.2 all-gather.4
  210.3 17.8 all-gather.8
  230.1 104.0 all-gather.10
  777.3 61.7 reduce-scatter.14
  842.6 67.5 reduce-scatter.12
  916.3 121.5 all-reduce.37
  1044.1 97.1 reduce-scatter.20
  1144.4 31.8 reduce-scatter.22
  1181.9 97.9 reduce-scatter.18
  1283.1 47.0 reduce-scatter.16
  1333.6 207.4 reduce-scatter.10
  1544.6 207.4 reduce-scatter.8
